TPU v7x, 256 devices: a whole 4x4x8 slice. The times are simulated.
256 devices in a mesh: req: 32 (over x, y, core), tp: 8 (over z).
Axes of the slice: x: 4, y: 4, z: 8, core: 2. Of those that a mesh axis runs over, the one named last changes fastest.
Arguments:
- query: bfloat16 [768, 4096], P('req', 'tp'), may hold values from -102 to 102
- new_key: bfloat16 [768, 1024], P('req', 'tp'), may hold values from -6 to 6
- new_value: bfloat16 [768, 1024], P('req', 'tp'), may hold values from -6 to 6
- prefix_key: bfloat16 [64, 6144, 1024], P('req', None, 'tp'), may hold values from -6 to 6
- prefix_value: bfloat16 [64, 6144, 1024], P('req', None, 'tp'), may hold values from -6 to 6
- suffix_key: bfloat16 [768, 128, 1024], P('req', None, 'tp'), may hold values from -6 to 6
- suffix_value: bfloat16 [768, 128, 1024], P('req', None, 'tp'), may hold values from -6 to 6
- group_ids: int32 [768], replicated, may hold values from 0 to 63, as said below
- prompt_len: int32 [64], P('req'), may hold values from 768 to 6144, as said below
- suffix_len: int32 [768], replicated, may hold values from 1 to 128, as said below
- o_weight: bfloat16 [4096, 4096], P('tp'), may hold values from -0.09375 to 0.09375
- residual: bfloat16 [768, 4096], P('req'), may hold values from -0.29882812 to 0.29882812
- norm_gain: bfloat16 [4096], replicated, may hold values from 0.5 to 1.5
Outputs:
- hidden: bfloat16 [768, 4096], P('req')
- normed: bfloat16 [768, 4096], P('req')
Inputs may be any that keep to these rules, and one draw needn't show every extreme that they name: Request r belongs to group group_ids[r]; groups 2k to 2k + 1 at a time are held together (group // 2 names the holder). Among each aligned block of 24 requests, every holder that appears is named by exactly 2 of them. `prompt_len`: some group has exactly 6144. `suffix_len`: some request has exactly 128.
All inputs are finite; a program needn't handle non-finite values.
Results may differ from a plain program's by a relative error of at most 0.008.
Values may be sent and summed in bfloat16 or wider, within the bound.
No kernel may reach another device: no remote copies, remote signals or barrier semaphores. Data moves between devices by JAX's collectives and lax.ppermute only.
A program may use at most 64 MiB of HBM per device.

v0:
```python
import math
import jax
import jax.numpy as jnp
from jax import lax
from jax.sharding import PartitionSpec as P

HD = 128
WIN = 4096
SINKS = 4
FAR_BELOW = -1e30
NORM_EPS = 1e-06


def prefix_attend(
    rows_query, row_group, row_suffix, prefix_key, prefix_value, prompt_len, first_group, blocks
):
    row_count = rows_query.shape[0]
    groups_dev = prefix_key.shape[0]
    prompt_max = prefix_key.shape[1]
    kv_dev = prefix_key.shape[2] // HD
    heads_dev = rows_query.shape[1] // HD
    repeat = heads_dev // kv_dev
    block_len = min(512, prompt_max)
    score_scale = 1.0 / math.sqrt(HD)
    local_group = row_group - first_group
    owned = (local_group >= 0) & (local_group < groups_dev)
    member = local_group[:, None] == jnp.arange(groups_dev, dtype=jnp.int32)[None, :]
    row_prompt = jnp.sum(jnp.where(member, prompt_len[None, :], 0), axis=1)
    row_low = row_prompt + row_suffix - WIN + 1
    queries = rows_query.reshape(row_count, kv_dev, repeat, HD)

    def key_step(block_index, loop_state):
        running, weight_sum, weighted = loop_state
        key_start = block_index * block_len
        key_block = lax.dynamic_slice_in_dim(prefix_key, key_start, block_len, 1).reshape(
            groups_dev, block_len, kv_dev, HD
        )
        value_block = lax.dynamic_slice_in_dim(prefix_value, key_start, block_len, 1).reshape(
            groups_dev, block_len, kv_dev, HD
        )
        scores = (
            jnp.einsum("rkhd,gpkd->rkhgp", queries, key_block, preferred_element_type=jnp.float32)
            * score_scale
        )
        positions = key_start + jnp.arange(block_len, dtype=jnp.int32)
        inside = positions[None, :] < prompt_len[:, None]
        window = (positions[None, :] < SINKS) | (positions[None, :] >= row_low[:, None])
        usable = member[:, :, None] & inside[None, :, :] & window[:, None, :]
        usable = usable[:, None, None, :, :]
        masked = jnp.where(usable, scores, FAR_BELOW)
        updated = jnp.maximum(running, jnp.max(masked, axis=(3, 4)))
        weights = jnp.where(usable, jnp.exp(masked - updated[..., None, None]), 0.0)
        rescale = jnp.exp(running - updated)
        weight_sum = weight_sum * rescale + jnp.sum(weights, axis=(3, 4))
        rounded = weights.astype(jnp.bfloat16)
        weighted = weighted * rescale[..., None] + jnp.einsum(
            "rkhgp,gpkd->rkhd", rounded, value_block, preferred_element_type=jnp.float32
        )
        return (updated, weight_sum, weighted)

    initial = (
        jnp.full((row_count, kv_dev, repeat), FAR_BELOW, jnp.float32),
        jnp.zeros((row_count, kv_dev, repeat), jnp.float32),
        jnp.zeros((row_count, kv_dev, repeat, HD), jnp.float32),
    )
    running, weight_sum, weighted = lax.fori_loop(0, blocks, key_step, initial)
    bounded = jnp.maximum(weight_sum, 1.0)
    normalized = jnp.where(owned[:, None, None, None], weighted / bounded[..., None], 0.0).reshape(
        row_count, heads_dev * HD
    )
    log_total = jnp.where(owned[:, None, None], running + jnp.log(bounded), 0.0).reshape(
        row_count, heads_dev
    )
    return (normalized, log_total)


def body(
    query,
    new_key,
    new_value,
    prefix_key,
    prefix_value,
    suffix_key,
    suffix_value,
    group_ids,
    prompt_len,
    suffix_len,
    o_weight,
    residual,
    norm_gain,
):
    req_dev = query.shape[0]
    heads_dev = query.shape[1] // HD
    kv_dev = new_key.shape[1] // HD
    repeat = heads_dev // kv_dev
    groups_dev = prefix_key.shape[0]
    prompt_max = prefix_key.shape[1]
    suffix_max = suffix_key.shape[1]
    block_len = min(512, prompt_max)
    score_scale = 1.0 / math.sqrt(HD)
    places = lax.axis_size("req")
    device = lax.axis_index("req")
    first_group = device * groups_dev
    own_suffix = lax.dynamic_slice_in_dim(suffix_len, device * req_dev, req_dev)
    blocks = prompt_max // block_len
    capacity = max(2, req_dev // places)
    slot_total = places * capacity
    all_groups = group_ids.reshape(places, 1, req_dev)
    all_suffix = suffix_len.reshape(places, 1, req_dev)
    all_rows = (
        jnp.arange(places, dtype=jnp.int32)[:, None] * req_dev
        + jnp.arange(req_dev, dtype=jnp.int32)[None, :]
    ).reshape(places, 1, req_dev)
    is_mine = (group_ids // groups_dev).reshape(places, req_dev) == device
    slot_order = jnp.cumsum(is_mine.astype(jnp.int32), axis=1) - 1
    slot_pick = is_mine[:, None, :] & (
        slot_order[:, None, :] == jnp.arange(capacity, dtype=jnp.int32)[None, :, None]
    )
    filled = jnp.any(slot_pick, axis=2)
    slot_group = jnp.where(
        filled, jnp.sum(jnp.where(slot_pick, all_groups, 0), axis=2), -1
    ).reshape(slot_total)
    slot_suffix = jnp.sum(jnp.where(slot_pick, all_suffix, 0), axis=2).reshape(slot_total)
    slot_row = jnp.where(filled, jnp.sum(jnp.where(slot_pick, all_rows, 0), axis=2), -1).reshape(
        slot_total
    )
    every_query = lax.all_gather(query, "req", axis=0, tiled=True)
    pick_rows = slot_row[:, None] == jnp.arange(places * req_dev, dtype=jnp.int32)[None, :]
    compact = jnp.dot(
        pick_rows.astype(jnp.bfloat16), every_query, preferred_element_type=jnp.float32
    ).astype(jnp.bfloat16)
    part_out, part_log = prefix_attend(
        compact, slot_group, slot_suffix, prefix_key, prefix_value, prompt_len, first_group, blocks
    )
    spread_rows = pick_rows.T.astype(jnp.float32)
    spread_out = jnp.dot(spread_rows, part_out, precision=lax.Precision.HIGHEST)
    spread_log = jnp.dot(spread_rows, part_log, precision=lax.Precision.HIGHEST)
    prefix_out, prefix_log = (
        lax.psum_scatter(spread_out, "req", scatter_dimension=0, tiled=True),
        lax.psum_scatter(spread_log, "req", scatter_dimension=0, tiled=True),
    )
    queries = query.reshape(req_dev, kv_dev, repeat, HD)
    key_rows = suffix_key.reshape(req_dev, suffix_max, kv_dev, HD)
    value_rows = suffix_value.reshape(req_dev, suffix_max, kv_dev, HD)
    scores = (
        jnp.einsum("rkhd,rjkd->rkhj", queries, key_rows, preferred_element_type=jnp.float32)
        * score_scale
    )
    own_score = (
        jnp.einsum(
            "rkhd,rkd->rkh",
            queries,
            new_key.reshape(req_dev, kv_dev, HD),
            preferred_element_type=jnp.float32,
        )
        * score_scale
    )
    usable = (jnp.arange(suffix_max, dtype=jnp.int32)[None, :] < own_suffix[:, None])[
        :, None, None, :
    ]
    masked = jnp.where(usable, scores, FAR_BELOW)
    running = jnp.maximum(jnp.max(masked, axis=-1), own_score)
    weights = jnp.where(usable, jnp.exp(masked - running[..., None]), 0.0)
    own_weight = jnp.exp(own_score - running)
    weight_sum = jnp.sum(weights, axis=-1) + own_weight
    weighted = jnp.einsum(
        "rkhj,rjkd->rkhd",
        weights.astype(jnp.bfloat16),
        value_rows,
        preferred_element_type=jnp.float32,
    )
    own_rounded = own_weight.astype(jnp.bfloat16).astype(jnp.float32)
    weighted = weighted + own_rounded[..., None] * new_value.reshape(req_dev, kv_dev, 1, HD).astype(
        jnp.float32
    )
    local_out = weighted / weight_sum[..., None]
    local_log = running + jnp.log(weight_sum)
    prefix_out = prefix_out.reshape(req_dev, kv_dev, repeat, HD)
    prefix_log = prefix_log.reshape(req_dev, kv_dev, repeat)
    combined = jnp.logaddexp(prefix_log, local_log)
    attended = (
        prefix_out * jnp.exp(prefix_log - combined)[..., None]
        + local_out * jnp.exp(local_log - combined)[..., None]
    )
    attended = attended.reshape(req_dev, heads_dev * HD).astype(jnp.bfloat16)
    partial_value = jnp.dot(attended, o_weight, preferred_element_type=jnp.float32)
    proj = lax.psum(partial_value, "tp")
    summed = residual.astype(jnp.float32) + proj
    hidden = summed.astype(jnp.bfloat16)
    inverse = lax.rsqrt(jnp.mean(summed * summed, axis=-1, keepdims=True) + NORM_EPS)
    normed = (summed * inverse * norm_gain.astype(jnp.float32)[None, :]).astype(jnp.bfloat16)
    return (hidden, normed)


def solution(mesh):
    placed = (
        P("req", "tp"),
        P("req", "tp"),
        P("req", "tp"),
        P("req", None, "tp"),
        P("req", None, "tp"),
        P("req", None, "tp"),
        P("req", None, "tp"),
        P(),
        P("req"),
        P(),
        P("tp", None),
        P("req", None),
        P(),
    )
    return jax.shard_map(
        body,
        mesh=mesh,
        in_specs=placed,
        out_specs=(P("req", None), P("req", None)),
        check_vma=False,
    )
```

profile of v0, /device:TPU:2, one launch (start us, length us, event | category | flops | bytes accessed | tf_op | source)
XLA Modules:
  0.0 305.6 jit_solution(10688126659396240701)
XLA Ops:
  7.3 0.8 fusion.51
  8.2 0.8 broadcast_in_dim.180
  9.3 0.8 broadcast_in_dim.188
  10.5 0.7 fusion.59
  11.4 24.9 %all_gather.3 = bf16[768,512]{1,0:T(8,128)(2,1)S(1)} all-gather(bf16[24,512]{1,0:T(8,128)(2,1)} %param.15), channel_id=1, replica_groups=mesh['req'=32,'tp'=8] {'req'}, dimensions={0}, use_global_device_ids=true | all-gather | bytes 811008 | tf_op jit(solution)/shard_map/all_gather | solution.py:127
  36.8 50.0 %while.18 = (s32[]{:T(128)}, f32[64,1,4]{0,2,1:T(4,128)S(1)}, f32[64,1,4]{0,2,1:T(4,128)S(1)}, f32[64,1,4,128]{3,0,2,1:T(8,128)S(1)}, s32[2]{0:T(128)}, /*index=...) while((s32[]{:T(128)}, f32[64,1,4]{0,2,1:T(4,128)S(1)}, ...), condition=%wide.region_9.10_spmd.clone, body=%wide.region_6.9_spmd.clone.sunk | while | flops 136876160 | bytes 4351967 | solution.py:66
  37.0 0.7 broadcast_compare_fusion.5
  37.8 1.4 fusion.83
  39.6 1.4 fusion.86
  41.2 0.7 broadcast_compare_fusion.5
  42.0 1.4 fusion.83
  43.8 1.4 fusion.86
  45.3 0.7 broadcast_compare_fusion.5
  46.2 1.4 fusion.83
  47.9 1.4 fusion.86
  49.5 0.7 broadcast_compare_fusion.5
  50.3 1.4 fusion.83
  52.1 1.4 fusion.86
  53.7 0.7 broadcast_compare_fusion.5
  54.5 1.4 fusion.83
  56.3 1.4 fusion.86
  57.8 0.7 broadcast_compare_fusion.5
  58.7 1.4 fusion.83
  60.5 1.4 fusion.86
  62.0 0.7 broadcast_compare_fusion.5
  62.9 1.4 fusion.83
  64.6 1.4 fusion.86
  66.2 0.7 broadcast_compare_fusion.5
  67.0 1.4 fusion.83
  68.8 1.4 fusion.86
  70.3 0.7 broadcast_compare_fusion.5
  71.2 1.4 fusion.83
  73.0 1.4 fusion.86
  75.4 1.4 fusion.83
  77.1 1.4 fusion.86
  78.7 0.7 broadcast_compare_fusion.5
  79.5 1.4 fusion.83
  81.3 1.4 fusion.86
  83.7 1.4 fusion.83
  85.5 1.4 fusion.86
  87.2 2.0 fusion.27
  89.3 0.8 dynamic_slice.17
  91.6 109.0 %all-reduce = f32[768,4]{0,1:T(4,128)S(1)} all-reduce(f32[768,4]{0,1:T(4,128)S(1)} %fusion.26), channel_id=3, replica_groups=mesh['req'=32,'tp'=8] {'req'}, use_global_device_ids=true, to_apply=%region_11.12.clone | all-reduce | flops 3072 | bytes 24576
  201.9 0.8 reshape.377
  203.2 3.6 %fusion.37 = f32[24,4096]{1,0:T(8,128)} fusion(bf16[512,4096]{1,0:T(8,128)(2,1)} %param.25, bf16[3,8,4,128]{3,2,1,0:T(4,128)(2,1)S(1)} %bitcast.93), kind=kOutput, calls=%fused_computation.57 | convolution fusion | flops 100663296 | bytes 4612096 | tf_op jit(solution)/shard_map/dot_general | solution.py:186
  206.8 88.9 %all-reduce.3.cloned.1.call-done = f32[24,4096]{1,0:T(8,128)} async-done(((f32[24,4096]{1,0:T(8,128)}), f32[24,4096]{1,0:T(8,128)}) %all-reduce.3.cloned.1.call-update) | async-done | bytes 393232 | tf_op jit(solution)/shard_map/psum | solution.py:187
  295.8 1.2 multiply_reduce_fusion
  297.0 1.8 multiply_convert_fusion
  (177 shorter events, 13.2 us)
Async XLA Ops:
  7.2 193.8 %copy-start = (bf16[24,128,128]{2,1,0:T(8,128)(2,1)S(1)}, bf16[24,128,128]{2,1,0:T(8,128)(2,1)}, u32[]{:S(2)}) copy-start(bf16[24,128,128]{2,1,0:T(8,128)(2,1)} %param.20) | copy-start | bytes 2359300
  7.2 194.8 %reduce-scatter.3.cloned.1.call-start = ((), (), s32[]{:S(2)}) async-start(), calls=%async_computation.1 | async-start | bytes 1622016 | tf_op jit(solution)/shard_map/reduce_scatter | solution.py:139
  86.9 2.4 copy-start.2
  86.9 3.2 %copy-start.7 = (u32[256]{0:T(256)S(1)}, u32[256]{0:T(256)}, u32[]{:S(2)}) copy-start(u32[256]{0:T(256)} %constant.130) | copy-start | bytes 3076
  86.9 113.9 %copy-start.4 = (bf16[24,128]{1,0:T(8,128)(2,1)S(1)}, bf16[24,128]{1,0:T(8,128)(2,1)}, u32[]{:S(2)}) copy-start(bf16[24,128]{1,0:T(8,128)(2,1)} %param.17) | copy-start | bytes 18436
  86.9 113.9 %copy-start.6 = (bf16[24,128]{1,0:T(8,128)(2,1)S(1)}, bf16[24,128]{1,0:T(8,128)(2,1)}, u32[]{:S(2)}) copy-start(bf16[24,128]{1,0:T(8,128)(2,1)} %param.16) | copy-start | bytes 18436
  86.9 115.8 %copy-start.5 = (bf16[24,128,128]{2,1,0:T(8,128)(2,1)S(1)}, bf16[24,128,128]{2,1,0:T(8,128)(2,1)}, u32[]{:S(2)}) copy-start(bf16[24,128,128]{2,1,0:T(8,128)(2,1)} %param.21) | copy-start | bytes 2359300
  89.2 206.5 %all-reduce.3.cloned.1.call-start = ((), (), s32[]{:S(2)}) async-start(), calls=%async_computation.2 | async-start | bytes 786432 | tf_op jit(solution)/shard_map/psum | solution.py:187
  202.8 4.0 %copy-start.3 = (bf16[4096]{0:T(1024)(128)(2,1)S(1)}, bf16[4096]{0:T(1024)(128)(2,1)}, u32[]{:S(2)}) copy-start(bf16[4096]{0:T(1024)(128)(2,1)} %param.27) | copy-start | bytes 24580
  202.8 93.0 %copy-start.1 = (bf16[24,4096]{1,0:T(8,128)(2,1)S(1)}, bf16[24,4096]{1,0:T(8,128)(2,1)}, u32[]{:S(2)}) copy-start(bf16[24,4096]{1,0:T(8,128)(2,1)} %param.26) | copy-start | bytes 589828
Sparse Core Ops, SparseCore 0:
  89.4 86.8 reduce-scatter.2
  206.9 88.8 all-reduce.2
where the time goes:
time: 307 us; the launch traced here: 306 us
  blocking collectives  134 us (44%)
  waiting for transfers between devices  89 us (29%)
  matrix products  40.4 us (13%)
  other arithmetic  21.3 us (7%)
  between operations  15 us (5%)
  local copies, waits for them, and re-layouts  5.04 us (2%)
    unnamed x1, blocking collectives  109 us
    psum x1, waiting for transfers between devices, body(): proj = lax.psum(partial_value, 'tp')  88.9 us
    all_gather x1, blocking collectives, body(): every_query = lax.all_gather(query, 'req', axis=0, tiled=True)  24.9 us
    dot_general x12, matrix products, key_step(): jnp.einsum('rkhgp,gpkd->rkhd', rounded, value_block, preferred_element_ty...  16.8 us
    dot_general x12, matrix products, key_step(): jnp.einsum('rkhd,gpkd->rkhgp', queries, key_block, preferred_element_type...  16.3 us
    lt x12, other arithmetic, key_step(): inside = positions[None, :] < prompt_len[:, None]  8.77 us
  transfers between devices with their start and end apart: 2, of which 1 were waited for; matrix products, arithmetic and copies ran while one was open for 1% of the time, Pallas kernels for 0%

commit v1 on v0

--- a/solution.py
+++ b/solution.py
@@ -3,6 +3,7 @@
 import jax.numpy as jnp
 from jax import lax
 from jax.sharding import PartitionSpec as P
+from jax.lax import all_to_all, axis_size
 
 HD = 128
 WIN = 4096
@@ -124,7 +125,16 @@
     slot_row = jnp.where(filled, jnp.sum(jnp.where(slot_pick, all_rows, 0), axis=2), -1).reshape(
         slot_total
     )
-    every_query = lax.all_gather(query, "req", axis=0, tiled=True)
+    time_node = lambda target, peer_axis, along_dim: jnp.concatenate(
+        all_to_all(
+            jnp.stack([target] * axis_size(peer_axis)),
+            axis_name=peer_axis,
+            concat_axis=0,
+            split_axis=0,
+        ),
+        axis=along_dim,
+    )
+    every_query = time_node(query, "req", 0)
     pick_rows = slot_row[:, None] == jnp.arange(places * req_dev, dtype=jnp.int32)[None, :]
     compact = jnp.dot(
         pick_rows.astype(jnp.bfloat16), every_query, preferred_element_type=jnp.float32

time: 307 us -> 292 us (0.951)
  blocking collectives: 134 us -> 110 us
  other arithmetic: 21.3 us -> 13.3 us
  waiting for transfers between devices: 89 us -> 96.8 us
  starting transfers between devices: 0.08 us -> 7.7 us
    all_gather x1 -> x0, blocking collectives: 24.9 us -> none  [body(): every_query = lax.all_gather(query, 'req', axis=0, tiled=True)]
    lt x12, other arithmetic: 8.77 us -> 0.89 us  [key_step(): inside = positions[None, :] < prompt_len[:, None]]
    all_to_all x0 -> x1, waiting for transfers between devices: none -> 7.68 us  [body(): all_to_all(jnp.stack([target] * axis_size(peer_axis)), axis_name=peer_axi...]
    all_to_all x0 -> x1, starting transfers between devices: none -> 7.62 us  [body(): all_to_all(jnp.stack([target] * axis_size(peer_axis)), axis_name=peer_axi...]
  transfers between devices with their start and end apart: 2 -> 3, of which waited for: 1 -> 2; matrix products, arithmetic and copies ran while one was open for 1% -> 2% of each run, Pallas kernels for 0% -> 0%
where the time goes in v1:
time: 292 us; the launch traced here: 291 us
  blocking collectives  110 us (38%)
  waiting for transfers between devices  96.8 us (33%)
  matrix products  40.4 us (14%)
  between operations  15 us (5%)
  other arithmetic  13.3 us (5%)
  starting transfers between devices  7.7 us (3%)
  local copies, waits for them, and re-layouts  6.8 us (2%)
    unnamed x1, blocking collectives  110 us
    psum x1, waiting for transfers between devices, body(): proj = lax.psum(partial_value, 'tp')  89.1 us
    dot_general x12, matrix products, key_step(): jnp.einsum('rkhgp,gpkd->rkhd', rounded, value_block, preferred_element_ty...  16.8 us
    dot_general x12, matrix products, key_step(): jnp.einsum('rkhd,gpkd->rkhgp', queries, key_block, preferred_element_type...  16.3 us
    all_to_all x1, waiting for transfers between devices, body(): all_to_all(jnp.stack([target] * axis_size(peer_axis)), axis_name=peer_axi...  7.68 us
    all_to_all x1, starting transfers between devices, body(): all_to_all(jnp.stack([target] * axis_size(peer_axis)), axis_name=peer_axi...  7.62 us
  transfers between devices with their start and end apart: 3, of which 2 were waited for; matrix products, arithmetic and copies ran while one was open for 2% of the time, Pallas kernels for 0%

profile of v1, /device:TPU:2, one launch (start us, length us, event | category | flops | bytes accessed | tf_op | source)
XLA Modules:
  0.0 290.8 jit_solution(12943070124509745079)
XLA Ops:
  7.2 1.7 stack.2
  8.9 7.6 %all-to-all-start = ((bf16[32,24,512]{2,1,0:T(8,128)(2,1)}), bf16[32,24,512]{2,1,0:T(8,128)(2,1)S(1)}, u32[]{:S(2)}, u32[]{:S(2)}) async-start(bf16[32,24,512]{2,1,0:T(8,128)(2,1)} %stack.2), calls=%async_computation | async-start | bytes 1572864 | tf_op jit(solution)/shard_map/all_to_all | solution.py:129
  16.6 0.7 fusion.51
  17.5 0.8 broadcast_in_dim.180
  18.6 0.8 broadcast_in_dim.188
  20.2 0.7 fusion.59
  20.9 7.7 %all-to-all-done = bf16[32,24,512]{2,1,0:T(8,128)(2,1)S(1)} async-done(((bf16[32,24,512]{2,1,0:T(8,128)(2,1)}), bf16[32,24,512]{2,1,0:T(8,128)(2,1)S(1)}, u32[]{:S(2)}, u32[]{:S(2)}) %all-to-all-start) | async-done | bytes 786464 | tf_op jit(solution)/shard_map/all_to_all | solution.py:129
  29.0 42.2 %while.18 = (s32[]{:T(128)}, f32[64,1,4]{0,2,1:T(4,128)S(1)}, f32[64,1,4]{0,2,1:T(4,128)S(1)}, f32[64,1,4,128]{3,0,2,1:T(8,128)S(1)}, s32[2]{0:T(128)S(1)}, /*in...) while((s32[]{:T(128)}, f32[64,1,4]{0,2,1:T(4,128)S(1)}, ...), condition=%wide.region_9.10_spmd.clone, body=%wide.region_6.9_spmd.clone.sunk | while | flops 136876160 | bytes 4351967 | solution.py:67
  29.3 1.4 fusion.83
  30.7 0.4 fusion.85
  31.1 1.4 fusion.86
  32.8 1.4 fusion.83
  34.2 0.4 fusion.85
  34.6 1.4 fusion.86
  36.3 1.4 fusion.83
  37.7 0.4 fusion.85
  38.1 1.4 fusion.86
  39.9 1.4 fusion.83
  41.2 0.4 fusion.85
  41.6 1.4 fusion.86
  43.4 1.4 fusion.83
  44.8 0.4 fusion.85
  45.1 1.4 fusion.86
  46.9 1.4 fusion.83
  48.7 1.4 fusion.86
  50.4 1.4 fusion.83
  52.2 1.4 fusion.86
  53.9 1.4 fusion.83
  55.7 1.4 fusion.86
  57.4 1.4 fusion.83
  59.2 1.4 fusion.86
  60.9 1.4 fusion.83
  62.7 1.4 fusion.86
  64.5 1.4 fusion.83
  66.2 1.4 fusion.86
  68.0 1.4 fusion.83
  69.7 1.4 fusion.86
  71.4 2.0 fusion.27
  73.6 0.8 dynamic_slice.17
  74.4 0.6 dynamic-slice
  75.8 0.6 fusion.68
  76.9 109.8 %all-reduce = f32[768,4]{0,1:T(4,128)S(1)} all-reduce(f32[768,4]{0,1:T(4,128)S(1)} %fusion.26), channel_id=3, replica_groups=mesh['req'=32,'tp'=8] {'req'}, use_global_device_ids=true, to_apply=%region_11.12.clone | all-reduce | flops 3072 | bytes 24576
  187.0 0.8 reshape.383
  187.8 0.4 fusion.25
  188.2 3.6 %fusion.37 = f32[24,4096]{1,0:T(8,128)} fusion(bf16[512,4096]{1,0:T(8,128)(2,1)} %param.25, bf16[3,8,4,128]{3,2,1,0:T(4,128)(2,1)S(1)} %bitcast.95), kind=kOutput, calls=%fused_computation.57 | convolution fusion | flops 100663296 | bytes 4612096 | tf_op jit(solution)/shard_map/dot_general | solution.py:196
  191.9 89.1 %all-reduce.3.cloned.1.call-done = f32[24,4096]{1,0:T(8,128)} async-done(((f32[24,4096]{1,0:T(8,128)}), f32[24,4096]{1,0:T(8,128)}) %all-reduce.3.cloned.1.call-update) | async-done | bytes 393232 | tf_op jit(solution)/shard_map/psum | solution.py:197
  281.0 1.2 multiply_reduce_fusion
  282.1 1.8 multiply_convert_fusion
  (181 shorter events, 9.2 us)
Async XLA Ops:
  7.2 68.7 %copy-start = (bf16[24,128,128]{2,1,0:T(8,128)(2,1)S(1)}, bf16[24,128,128]{2,1,0:T(8,128)(2,1)}, u32[]{:S(2)}) copy-start(bf16[24,128,128]{2,1,0:T(8,128)(2,1)} %param.20) | copy-start | bytes 2359300
  7.2 21.8 %copy-start.3 = (s32[2]{0:T(128)S(1)}, s32[2]{0:T(128)}, u32[]{:S(2)}) copy-start(s32[2]{0:T(128)} %param.23) | copy-start | bytes 28
  8.9 19.7 %all-to-all-start = ((bf16[32,24,512]{2,1,0:T(8,128)(2,1)}), bf16[32,24,512]{2,1,0:T(8,128)(2,1)S(1)}, u32[]{:S(2)}, u32[]{:S(2)}) async-start(bf16[32,24,512]{2,1,0:T(8,128)(2,1)} %stack.2), calls=%async_computation | async-start | bytes 1572864 | tf_op jit(solution)/shard_map/all_to_all | solution.py:129
  16.6 170.4 %reduce-scatter.3.cloned.1.call-start = ((), (), s32[]{:S(2)}) async-start(), calls=%async_computation.2 | async-start | bytes 1622016 | tf_op jit(solution)/shard_map/reduce_scatter | solution.py:149
  71.2 2.4 copy-start.2
  71.2 3.2 %copy-start.5 = (bf16[24,128]{1,0:T(8,128)(2,1)S(1)}, bf16[24,128]{1,0:T(8,128)(2,1)}, u32[]{:S(2)}) copy-start(bf16[24,128]{1,0:T(8,128)(2,1)} %param.17) | copy-start | bytes 18436
  71.2 3.2 %copy-start.8 = (u32[256]{0:T(256)S(1)}, u32[256]{0:T(256)}, u32[]{:S(2)}) copy-start(u32[256]{0:T(256)} %constant.130) | copy-start | bytes 3076
  71.2 4.5 %copy-start.7 = (bf16[24,128]{1,0:T(8,128)(2,1)S(1)}, bf16[24,128]{1,0:T(8,128)(2,1)}, u32[]{:S(2)}) copy-start(bf16[24,128]{1,0:T(8,128)(2,1)} %param.16) | copy-start | bytes 18436
  71.2 116.6 %copy-start.6 = (bf16[24,128,128]{2,1,0:T(8,128)(2,1)S(1)}, bf16[24,128,128]{2,1,0:T(8,128)(2,1)}, u32[]{:S(2)}) copy-start(bf16[24,128,128]{2,1,0:T(8,128)(2,1)} %param.21) | copy-start | bytes 2359300
  73.5 207.4 %all-reduce.3.cloned.1.call-start = ((), (), s32[]{:S(2)}) async-start(), calls=%async_computation.3 | async-start | bytes 786432 | tf_op jit(solution)/shard_map/psum | solution.py:197
  187.8 4.0 %copy-start.4 = (bf16[4096]{0:T(1024)(128)(2,1)S(1)}, bf16[4096]{0:T(1024)(128)(2,1)}, u32[]{:S(2)}) copy-start(bf16[4096]{0:T(1024)(128)(2,1)} %param.27) | copy-start | bytes 24580
  187.8 93.1 %copy-start.1 = (bf16[24,4096]{1,0:T(8,128)(2,1)S(1)}, bf16[24,4096]{1,0:T(8,128)(2,1)}, u32[]{:S(2)}) copy-start(bf16[24,4096]{1,0:T(8,128)(2,1)} %param.26) | copy-start | bytes 589828
Sparse Core Ops, SparseCore 0:
  73.6 87.0 reduce-scatter.2
  192.0 88.9 all-reduce.2
